TPU v7x, 256 devices: a whole 4x4x8 slice. The times are simulated.
256 devices in a mesh: dp: 16 (over y_hi, z), seq: 16 (over x, y_lo, core).
Axes of the slice: x: 4, y: 4 (y_hi: 2, y_lo: 2; y = y_hi * 2 + y_lo), z: 8, core: 2. Of those that a mesh axis runs over, the one named last changes fastest.
Arguments:
- queries: bfloat16 [16, 2048, 2048], P('dp', 'seq'), may hold values from -6 to 6
- key_states: bfloat16 [16, 2048, 2048], P('dp', 'seq'), may hold values from -6 to 6
- value_states: bfloat16 [16, 2048, 2048], P('dp', 'seq'), may hold values from -6 to 6
- cotangent: bfloat16 [16, 2048, 2048], P('dp', 'seq'), may hold values from -6 to 6
- filter_taps: float32 [7, 2048], replicated, may hold values from -3 to 3
Outputs:
- conv_output: bfloat16 [16, 2048, 2048], P('dp', 'seq')
- grad_queries: bfloat16 [16, 2048, 2048], P('dp', 'seq')
- grad_keys: bfloat16 [16, 2048, 2048], P('dp', 'seq')
- grad_values: bfloat16 [16, 2048, 2048], P('dp', 'seq')
- filter_gradient: float32 [7, 2048], replicated
All inputs are finite; a program needn't handle non-finite values.
Results may differ from a plain program's by a relative error of at most 0.015.
Values may be sent and summed in bfloat16 or wider, within the bound.
No kernel may reach another device: no remote copies, remote signals or barrier semaphores. Data moves between devices by JAX's collectives and lax.ppermute only.
A program may use at most 128 MiB of HBM per device.

v0:
```python
import math
import jax
import jax.numpy as jnp
import numpy as np
from jax import lax
from jax.sharding import Mesh
from jax.sharding import PartitionSpec as P

HD = 128
TAPS = 7
GROUP_HEADS = 2
SEQ = ("sc", "core")


def padded(value, width):
    peers = lax.axis_size("sc") * lax.axis_size("core")
    length = value.shape[0]
    up = [(i, (i + 1) % peers) for i in range(peers)]
    down = [(j, i) for i, j in up]
    before = lax.ppermute(value[length - width :], SEQ, up)
    after = lax.ppermute(value[:width], SEQ, down)
    return jnp.concatenate([before, value, after], axis=0)


def to_chip_rows(value):
    rows, channels = value.shape
    split = value.reshape(rows, 2, channels // 2)
    return lax.all_to_all(split, "core", 1, 0, tiled=True).reshape(2 * rows, channels // 2)


def from_chip_rows(value):
    rows2, half = value.shape
    split = value.reshape(2, rows2 // 2, 1, half)
    out = lax.all_to_all(split, "core", 0, 2, tiled=True)
    return out.reshape(rows2 // 2, 2 * half)


def on_device(queries, key_states, value_states, cotangent, filter_taps):
    tok_rows = queries.shape[1]
    channels = queries.shape[2]
    chips = lax.axis_size("sc")
    seq_total = tok_rows * chips * 2
    chip_rows = 2 * tok_rows
    half_channels = channels // 2
    head_count = half_channels // HD
    group_width = GROUP_HEADS * HD
    group_count = head_count // GROUP_HEADS
    score_scale = HD ** (-0.5)
    half_width = (TAPS - 1) // 2
    local_q = queries[0]
    local_k = key_states[0]
    local_v = value_states[0]
    local_g = cotangent[0]
    grad_pad = padded(local_g, half_width)
    grad_sum = jnp.zeros((tok_rows, channels), jnp.float32)
    for tap_index in range(TAPS):
        start_row = 2 * half_width - tap_index
        grad_sum = grad_sum + filter_taps[tap_index] * grad_pad[
            start_row : start_row + tok_rows
        ].astype(jnp.float32)
    grad_attn = grad_sum.astype(jnp.bfloat16)
    chip_q = to_chip_rows(local_q)
    chip_k = to_chip_rows(local_k)
    chip_v = to_chip_rows(local_v)
    chip_d = to_chip_rows(grad_attn)
    chip_index = lax.axis_index("sc")
    query_pos = chip_index * chip_rows + jnp.arange(chip_rows, dtype=jnp.int32)
    key_pos = jnp.arange(seq_total, dtype=jnp.int32)
    visible = query_pos[:, None] >= key_pos[None, :]
    attended_parts, grad_q_parts, key_parts, value_parts = ([], [], [], [])
    for group_index in range(group_count):
        cols = slice(group_index * group_width, (group_index + 1) * group_width)
        k_all = lax.all_gather(chip_k[:, cols], "sc", axis=0, tiled=True)
        v_all = lax.all_gather(chip_v[:, cols], "sc", axis=0, tiled=True)
        q_part = chip_q[:, cols].reshape(chip_rows, GROUP_HEADS, HD)
        d_part = chip_d[:, cols].reshape(chip_rows, GROUP_HEADS, HD)
        k_part = k_all.reshape(seq_total, GROUP_HEADS, HD)
        v_part = v_all.reshape(seq_total, GROUP_HEADS, HD)
        scores = (
            jnp.einsum("thd,uhd->htu", q_part, k_part, preferred_element_type=jnp.float32)
            * score_scale
        )
        row_top = jnp.max(jnp.where(visible, scores, -jnp.inf), -1, keepdims=True)
        raw = jnp.where(visible, jnp.exp(scores - row_top), 0.0)
        row_total = jnp.sum(raw, -1, keepdims=True)
        probs = raw / row_total
        probs_low = probs.astype(jnp.bfloat16)
        attended = jnp.einsum("htu,uhd->thd", probs_low, v_part, preferred_element_type=jnp.float32)
        attended_parts.append(attended.astype(jnp.bfloat16).reshape(chip_rows, group_width))
        dprob = jnp.einsum("thd,uhd->htu", d_part, v_part, preferred_element_type=jnp.float32)
        row_delta = jnp.sum(probs * dprob, -1, keepdims=True)
        dscore = (probs * (dprob - row_delta) * score_scale).astype(jnp.bfloat16)
        grad_q = jnp.einsum("htu,uhd->thd", dscore, k_part, preferred_element_type=jnp.float32)
        grad_q_parts.append(grad_q.astype(jnp.bfloat16).reshape(chip_rows, group_width))
        key_term = jnp.einsum("htu,thd->uhd", dscore, q_part, preferred_element_type=jnp.float32)
        value_term = jnp.einsum(
            "htu,thd->uhd", probs_low, d_part, preferred_element_type=jnp.float32
        )
        key_parts.append(
            lax.psum_scatter(
                key_term.astype(jnp.bfloat16).reshape(seq_total, group_width),
                "sc",
                scatter_dimension=0,
                tiled=True,
            )
        )
        value_parts.append(
            lax.psum_scatter(
                value_term.astype(jnp.bfloat16).reshape(seq_total, group_width),
                "sc",
                scatter_dimension=0,
                tiled=True,
            )
        )
    attn_out = from_chip_rows(jnp.concatenate(attended_parts, axis=1))
    grad_queries = from_chip_rows(jnp.concatenate(grad_q_parts, axis=1))
    grad_keys = from_chip_rows(jnp.concatenate(key_parts, axis=1))
    grad_values = from_chip_rows(jnp.concatenate(value_parts, axis=1))
    out_pad = padded(attn_out, half_width)
    conv_sum = jnp.zeros((tok_rows, channels), jnp.float32)
    filter_rows = []
    local_gf = local_g.astype(jnp.float32)
    for tap_index in range(TAPS):
        moved = out_pad[tap_index : tap_index + tok_rows].astype(jnp.float32)
        conv_sum = conv_sum + filter_taps[tap_index] * moved
        filter_rows.append(jnp.sum(moved * local_gf, 0))
    filter_gradient = lax.psum(jnp.stack(filter_rows, 0), ("dp", "sc", "core"))
    conv_output = conv_sum.astype(jnp.bfloat16)
    return (
        conv_output[None],
        grad_queries[None],
        grad_keys[None],
        grad_values[None],
        filter_gradient,
    )


def solution(mesh):
    devices = np.asarray(mesh.devices)
    dp_size, seq_size = devices.shape
    split_mesh = Mesh(devices.reshape(dp_size, seq_size // 2, 2), ("dp", "sc", "core"))
    block = P("dp", SEQ, None)
    in_specs = (block, block, block, block, P())
    out_specs = (block, block, block, block, P())
    return jax.shard_map(
        on_device, mesh=split_mesh, in_specs=in_specs, out_specs=out_specs, check_vma=False
    )
```

profile of v0, /device:TPU:1, one launch (start us, length us, event | category | flops | bytes accessed | tf_op | source)
XLA Modules:
  0.0 740.7 jit_solution(332086236696625652)
XLA Ops:
  36.2 20.8 %collective-permute-done.2 = bf16[3,2048]{0,1:T(8,128)(2,1)S(1)} collective-permute-done((bf16[3,2048]{0,1:T(8,128)(2,1)}, bf16[3,2048]{0,1:T(8,128)(2,1)S(1)}, u32[]{:S(2)}, u32[]{:S(2)}) %collective-permute-start.2) | collective-permute-done | bytes 12320 | tf_op jit(solution)/shard_map/ppermute | solution.py:21
  71.0 34.5 %all-gather.15.cloned.1.call-done = bf16[2048,256]{1,0:T(8,128)(2,1)} async-done(((bf16[256,256]{1,0:T(8,128)(2,1)}), bf16[2048,256]{1,0:T(8,128)(2,1)}) %all-gather.15.cloned.1.call-update) | async-done | bytes 1048592 | tf_op jit(solution)/shard_map/all_gather | solution.py:74
  116.5 9.7 %convolution_convert_fusion.2 = bf16[2,2048,128]{1,2,0:T(8,128)(2,1)} fusion(bf16[256,2,128]{0,2,1:T(8,128)(2,1)} %bitcast.232, f32[2,256,2048]{2,1,0:T(8,128)} %fusion.183, f32[2,256,2048]{2,1,0:T(8,128)} %get-tuple-element.66, f32[2,256]{1,0:T(2,128)} %get-tuple-element.65), kind=kOutput, calls=%fused_computation.45 | convolution fusion | flops 276302336 | bytes 9570304 | tf_op jit(solution)/shard_map/htu,thd->uhd/dot_general | solution.py:95
  127.9 19.7 %all-gather.17.cloned.1.call-done = bf16[2048,256]{1,0:T(8,128)(2,1)} async-done(((bf16[256,256]{1,0:T(8,128)(2,1)}), bf16[2048,256]{1,0:T(8,128)(2,1)}) %all-gather.17.cloned.1.call-update) | async-done | bytes 1048592 | tf_op jit(solution)/shard_map/all_gather | solution.py:73
  149.9 41.5 %all-gather.19.cloned.1.call-done = bf16[2048,256]{1,0:T(8,128)(2,1)} async-done(((bf16[256,256]{1,0:T(8,128)(2,1)}), bf16[2048,256]{1,0:T(8,128)(2,1)}) %all-gather.19.cloned.1.call-update) | async-done | bytes 1048592 | tf_op jit(solution)/shard_map/all_gather | solution.py:74
  203.1 9.7 %convolution_convert_fusion.1 = bf16[2,2048,128]{1,2,0:T(8,128)(2,1)} fusion(bf16[256,2,128]{0,2,1:T(8,128)(2,1)} %bitcast.236, f32[2,256,2048]{2,1,0:T(8,128)} %fusion.184, f32[2,256,2048]{2,1,0:T(8,128)} %get-tuple-element.64, f32[2,256]{1,0:T(2,128)} %get-tuple-element.63), kind=kOutput, calls=%fused_computation.44 | convolution fusion | flops 276302336 | bytes 9570304 | tf_op jit(solution)/shard_map/htu,thd->uhd/dot_general | solution.py:95
  214.6 19.3 %all-gather.21.cloned.1.call-done = bf16[2048,256]{1,0:T(8,128)(2,1)} async-done(((bf16[256,256]{1,0:T(8,128)(2,1)}), bf16[2048,256]{1,0:T(8,128)(2,1)}) %all-gather.21.cloned.1.call-update) | async-done | bytes 1048592 | tf_op jit(solution)/shard_map/all_gather | solution.py:73
  236.1 41.4 %all-gather.23.cloned.1.call-done = bf16[2048,256]{1,0:T(8,128)(2,1)} async-done(((bf16[256,256]{1,0:T(8,128)(2,1)}), bf16[2048,256]{1,0:T(8,128)(2,1)}) %all-gather.23.cloned.1.call-update) | async-done | bytes 1048592 | tf_op jit(solution)/shard_map/all_gather | solution.py:74
  290.2 9.7 %convolution_convert_fusion = bf16[2,2048,128]{1,2,0:T(8,128)(2,1)} fusion(bf16[256,2,128]{0,2,1:T(8,128)(2,1)} %bitcast.238, f32[2,256,2048]{2,1,0:T(8,128)} %fusion.185, f32[2,256,2048]{2,1,0:T(8,128)} %get-tuple-element.62, f32[2,256]{1,0:T(2,128)} %get-tuple-element.61), kind=kOutput, calls=%fused_computation.43 | convolution fusion | flops 276302336 | bytes 9570304 | tf_op jit(solution)/shard_map/htu,thd->uhd/dot_general | solution.py:95
  301.1 18.5 %all-gather.9.cloned.1.call-done = bf16[2048,256]{1,0:T(8,128)(2,1)} async-done(((bf16[256,256]{1,0:T(8,128)(2,1)}), bf16[2048,256]{1,0:T(8,128)(2,1)}) %all-gather.9.cloned.1.call-update) | async-done | bytes 1048592 | tf_op jit(solution)/shard_map/all_gather | solution.py:73
  321.9 42.0 %all-gather.11.cloned.1.call-done = bf16[2048,256]{1,0:T(8,128)(2,1)} async-done(((bf16[256,256]{1,0:T(8,128)(2,1)}), bf16[2048,256]{1,0:T(8,128)(2,1)}) %all-gather.11.cloned.1.call-update) | async-done | bytes 1048592 | tf_op jit(solution)/shard_map/all_gather | solution.py:74
  376.0 9.6 %convolution_convert_fusion.3 = bf16[2,2048,128]{1,2,0:T(8,128)(2,1)} fusion(bf16[256,2,128]{0,2,1:T(8,128)(2,1)S(1)} %bitcast.234, f32[2,256,2048]{2,1,0:T(8,128)} %fusion.182, f32[2,256,2048]{2,1,0:T(8,128)} %get-tuple-element.68, f32[2,256]{1,0:T(2,128)S(1)} %get-tuple-element.67), kind=kOutput, calls=%fused_computation.46 | convolution fusion | flops 276302336 | bytes 9570304 | tf_op jit(solution)/shard_map/htu,thd->uhd/dot_general | solution.py:95
  396.6 8.2 %fusion.91 = bf16[256,2,128]{2,0,1:T(8,128)(2,1)S(1)} fusion(bf16[2048,2,128]{0,2,1:T(8,128)(2,1)} %bitcast.215, f32[2,256,2048]{2,1,0:T(8,128)} %fusion.183, f32[2,256,2048]{2,1,0:T(8,128)} %get-tuple-element.66, f32[2,256]{1,0:T(2,128)S(1)} %copy-done.23), kind=kOutput, calls=%fused_computation.111 | convolution fusion | flops 275843584 | bytes 9570304 | tf_op jit(solution)/shard_map/htu,uhd->thd/dot_general | solution.py:93
  412.7 7.9 %fusion.94 = bf16[256,2,128]{2,0,1:T(8,128)(2,1)S(1)} fusion(bf16[2048,2,128]{0,2,1:T(8,128)(2,1)S(1)} %bitcast.217, f32[2,256,2048]{2,1,0:T(8,128)} %fusion.184, f32[2,256,2048]{2,1,0:T(8,128)} %get-tuple-element.64, f32[2,256]{1,0:T(2,128)S(1)} %copy-done.24), kind=kOutput, calls=%fused_computation.112 | convolution fusion | flops 275843584 | bytes 9570304 | tf_op jit(solution)/shard_map/htu,uhd->thd/dot_general | solution.py:93
  429.3 8.1 %fusion.97 = bf16[256,2,128]{2,0,1:T(8,128)(2,1)S(1)} fusion(bf16[2048,2,128]{0,2,1:T(8,128)(2,1)S(1)} %bitcast.219, f32[2,256,2048]{2,1,0:T(8,128)} %fusion.185, f32[2,256,2048]{2,1,0:T(8,128)} %get-tuple-element.62, f32[2,256]{1,0:T(2,128)} %get-tuple-element.61), kind=kOutput, calls=%fused_computation.113 | convolution fusion | flops 275843584 | bytes 9570304 | tf_op jit(solution)/shard_map/htu,uhd->thd/dot_general | solution.py:93
  437.9 8.0 %fusion.88 = bf16[256,2,128]{2,0,1:T(8,128)(2,1)S(1)} fusion(bf16[2048,2,128]{0,2,1:T(8,128)(2,1)S(1)} %bitcast.221, f32[2,256,2048]{2,1,0:T(8,128)} %fusion.182, f32[2,256,2048]{2,1,0:T(8,128)} %get-tuple-element.68, f32[2,256]{1,0:T(2,128)} %copy-done.26), kind=kOutput, calls=%fused_computation.110 | convolution fusion | flops 275843584 | bytes 9570304 | tf_op jit(solution)/shard_map/htu,uhd->thd/dot_general | solution.py:93
  447.1 8.7 %all-to-all-start.3 = ((bf16[2,128,1,1024]{3,1,2,0:T(8,128)(2,1)}), bf16[2,128,1,1024]{3,1,2,0:T(8,128)(2,1)S(1)}, u32[]{:S(2)}, u32[]{:S(2)}) async-start(bf16[2,128,1,1024]{3,1,2,0:T(8,128)(2,1)} %maximum_bitcast_fusion), calls=%async_computation.3 | async-start | bytes 1048576 | tf_op jit(solution)/shard_map/all_to_all | solution.py:34
  464.4 7.4 collective-permute-done.1
  480.0 81.5 %psum.7 = f32[7,2048]{1,0:T(8,128)} all-reduce(f32[7,2048]{1,0:T(8,128)S(1)} %stack.31), channel_id=1, replica_groups=mesh['dp'=16,'sc'=8,'core'=2] {'dp','sc','core'}, use_global_device_ids=true, to_apply=%region_27.28 | all-reduce | flops 14336 | bytes 114688 | tf_op jit(solution)/shard_map/psum | solution.py:127
  563.0 23.9 %reduce-scatter.19.cloned.1.call-done = bf16[256,256]{0,1:T(8,128)(2,1)} async-done(((bf16[2048,256]{0,1:T(8,128)(2,1)}), bf16[256,256]{0,1:T(8,128)(2,1)}) %reduce-scatter.19.cloned.1.call-update) | async-done | bytes 131088 | tf_op jit(solution)/shard_map/reduce_scatter | solution.py:108
  586.8 43.3 %reduce-scatter.21.cloned.1.call-done = bf16[256,256]{0,1:T(8,128)(2,1)} async-done(((bf16[2048,256]{0,1:T(8,128)(2,1)}), bf16[256,256]{0,1:T(8,128)(2,1)}) %reduce-scatter.21.cloned.1.call-update) | async-done | bytes 131088 | tf_op jit(solution)/shard_map/reduce_scatter | solution.py:108
  630.1 43.4 %reduce-scatter.23.cloned.1.call-done = bf16[256,256]{0,1:T(8,128)(2,1)} async-done(((bf16[2048,256]{0,1:T(8,128)(2,1)}), bf16[256,256]{0,1:T(8,128)(2,1)}) %reduce-scatter.23.cloned.1.call-update) | async-done | bytes 131088 | tf_op jit(solution)/shard_map/reduce_scatter | solution.py:108
  673.5 43.4 %reduce-scatter.17.cloned.1.call-done = bf16[256,256]{0,1:T(8,128)(2,1)} async-done(((bf16[2048,256]{0,1:T(8,128)(2,1)}), bf16[256,256]{0,1:T(8,128)(2,1)}) %reduce-scatter.17.cloned.1.call-update) | async-done | bytes 131088 | tf_op jit(solution)/shard_map/reduce_scatter | solution.py:108
  718.3 9.0 %all_to_all.123 = bf16[2,128,1,1024]{3,1,2,0:T(8,128)(2,1)S(1)} all-to-all(bf16[2,128,1,1024]{3,1,2,0:T(8,128)(2,1)S(1)} %bitcast.199), channel_id=1, replica_groups=mesh['dp'=16,'sc'=8,'core'=2] {'core'}, dimensions={0} | all-to-all | bytes 1048576 | tf_op jit(solution)/shard_map/all_to_all | solution.py:34
  (195 shorter events, 156.8 us)
Async XLA Ops:
  7.2 62.3 %all-gather.13.cloned.1.call-start = ((), (), s32[]{:S(2)}) async-start(), calls=%async_computation.18 | async-start | bytes 1179648 | tf_op jit(solution)/shard_map/all_gather | solution.py:73
  16.8 88.7 %all-gather.15.cloned.1.call-start = ((), (), s32[]{:S(2)}) async-start(), calls=%async_computation.19 | async-start | bytes 1179648 | tf_op jit(solution)/shard_map/all_gather | solution.py:74
  22.4 125.3 %all-gather.17.cloned.1.call-start = ((), (), s32[]{:S(2)}) async-start(), calls=%async_computation.20 | async-start | bytes 1179648 | tf_op jit(solution)/shard_map/all_gather | solution.py:73
  23.1 168.3 %all-gather.19.cloned.1.call-start = ((), (), s32[]{:S(2)}) async-start(), calls=%async_computation.21 | async-start | bytes 1179648 | tf_op jit(solution)/shard_map/all_gather | solution.py:74
  23.7 210.2 %all-gather.21.cloned.1.call-start = ((), (), s32[]{:S(2)}) async-start(), calls=%async_computation.22 | async-start | bytes 1179648 | tf_op jit(solution)/shard_map/all_gather | solution.py:73
  24.3 253.2 %all-gather.23.cloned.1.call-start = ((), (), s32[]{:S(2)}) async-start(), calls=%async_computation.23 | async-start | bytes 1179648 | tf_op jit(solution)/shard_map/all_gather | solution.py:74
  24.8 294.7 %all-gather.9.cloned.1.call-start = ((), (), s32[]{:S(2)}) async-start(), calls=%async_computation.16 | async-start | bytes 1179648 | tf_op jit(solution)/shard_map/all_gather | solution.py:73
  26.6 8.0 %all-to-all-start = ((bf16[128,2,1024]{0,2,1:T(8,128)(2,1)}), bf16[128,2,1024]{0,2,1:T(8,128)(2,1)S(1)}, u32[]{:S(2)}, u32[]{:S(2)}) async-start(bf16[128,2,1024]{0,2,1:T(8,128)(2,1)} %bitcast.1), calls=%async_computation | async-start | bytes 1048576 | tf_op jit(solution)/shard_map/all_to_all | solution.py:28
  30.5 333.4 %all-gather.11.cloned.1.call-start = ((), (), s32[]{:S(2)}) async-start(), calls=%async_computation.17 | async-start | bytes 1179648 | tf_op jit(solution)/shard_map/all_gather | solution.py:74
  31.7 25.3 %collective-permute-start.2 = (bf16[3,2048]{0,1:T(8,128)(2,1)}, bf16[3,2048]{0,1:T(8,128)(2,1)S(1)}, u32[]{:S(2)}, u32[]{:S(2)}) collective-permute-start(bf16[3,2048]{0,1:T(8,128)(2,1)} %get-tuple-element.38), channel_id=1, source_target_pairs={{1,0},{2,1},{3,2},{4,3},{5,4},{6,5},{7,6},{8,7},{9,8},{10,9},{11,1... | collective-permute-start | bytes 36872 | tf_op jit(solution)/shard_map/ppermute | solution.py:21
  31.8 26.3 %collective-permute-start.3 = (bf16[3,2048]{0,1:T(8,128)(2,1)S(1)}, bf16[3,2048]{0,1:T(8,128)(2,1)}, u32[]{:S(2)}, u32[]{:S(2)}) collective-permute-start(bf16[3,2048]{0,1:T(8,128)(2,1)S(1)} %get-tuple-element.39), channel_id=1, source_target_pairs={{0,1},{1,2},{2,3},{3,4},{4,5},{5,6},{6,7},{7,8},{8,9},{9,10},{10,1... | collective-permute-start | bytes 36872 | tf_op jit(solution)/shard_map/ppermute | solution.py:20
  33.5 528.1 %reduce-scatter.11.cloned.1.call-start = ((), (), s32[]{:S(2)}) async-start(), calls=%async_computation.25 | async-start | bytes 1179648 | tf_op jit(solution)/shard_map/reduce_scatter | solution.py:100
  126.1 435.4 %reduce-scatter.13.cloned.1.call-start = ((), (), s32[]{:S(2)}) async-start(), calls=%async_computation.26 | async-start | bytes 1179648 | tf_op jit(solution)/shard_map/reduce_scatter | solution.py:100
  212.8 348.8 %reduce-scatter.15.cloned.1.call-start = ((), (), s32[]{:S(2)}) async-start(), calls=%async_computation.27 | async-start | bytes 1179648 | tf_op jit(solution)/shard_map/reduce_scatter | solution.py:100
  300.0 261.6 %reduce-scatter.9.cloned.1.call-start = ((), (), s32[]{:S(2)}) async-start(), calls=%async_computation.24 | async-start | bytes 1179648 | tf_op jit(solution)/shard_map/reduce_scatter | solution.py:100
  301.1 68.9 %copy-start.13 = (bf16[256,256]{0,1:T(8,128)(2,1)}, bf16[256,256]{0,1:T(8,128)(2,1)S(1)}, u32[]{:S(2)}) copy-start(bf16[256,256]{0,1:T(8,128)(2,1)S(1)} %copy.319) | copy-start | bytes 393220
  385.7 201.1 %reduce-scatter.19.cloned.1.call-start = ((), (), s32[]{:S(2)}) async-start(), calls=%async_computation.29 | async-start | bytes 1179648 | tf_op jit(solution)/shard_map/reduce_scatter | solution.py:108
  389.5 240.6 %reduce-scatter.21.cloned.1.call-start = ((), (), s32[]{:S(2)}) async-start(), calls=%async_computation.30 | async-start | bytes 1179648 | tf_op jit(solution)/shard_map/reduce_scatter | solution.py:108
  393.4 280.1 %reduce-scatter.23.cloned.1.call-start = ((), (), s32[]{:S(2)}) async-start(), calls=%async_computation.31 | async-start | bytes 1179648 | tf_op jit(solution)/shard_map/reduce_scatter | solution.py:108
  412.2 304.7 %reduce-scatter.17.cloned.1.call-start = ((), (), s32[]{:S(2)}) async-start(), calls=%async_computation.28 | async-start | bytes 1179648 | tf_op jit(solution)/shard_map/reduce_scatter | solution.py:108
  447.1 10.0 %all-to-all-start.3 = ((bf16[2,128,1,1024]{3,1,2,0:T(8,128)(2,1)}), bf16[2,128,1,1024]{3,1,2,0:T(8,128)(2,1)S(1)}, u32[]{:S(2)}, u32[]{:S(2)}) async-start(bf16[2,128,1,1024]{3,1,2,0:T(8,128)(2,1)} %maximum_bitcast_fusion), calls=%async_computation.3 | async-start | bytes 1048576 | tf_op jit(solution)/shard_map/all_to_all | solution.py:34
  457.1 5.6 all-to-all-start.5
  461.7 2.4 collective-permute-start
  461.7 10.0 %collective-permute-start.1 = (bf16[3,2048]{0,1:T(8,128)(2,1)S(1)}, bf16[3,2048]{0,1:T(8,128)(2,1)S(1)}, u32[]{:S(2)}, u32[]{:S(2)}) collective-permute-start(bf16[3,2048]{0,1:T(8,128)(2,1)S(1)} %bitcast.222), channel_id=1, source_target_pairs={{1,0},{2,1},{3,2},{4,3},{5,4},{6,5},{7,6},{8,7},{9,8},{10,9},{11,1... | collective-permute-start | bytes 36872 | tf_op jit(solution)/shard_map/ppermute | solution.py:21
  (27 other events, 320.9 us)
Sparse Core Ops, SparseCore 0:
  16.9 45.7 all-gather.12
  64.6 40.9 all-gather.14
  107.3 40.2 all-gather.16
  149.3 42.1 all-gather.18
  193.0 40.7 all-gather.20
  236.1 41.3 all-gather.22
  279.3 40.2 all-gather.8
  321.9 41.8 all-gather.10
  366.4 41.0 reduce-scatter.10
  409.8 41.1 reduce-scatter.12
  453.5 44.8 reduce-scatter.14
  500.8 42.3 reduce-scatter.8
  545.8 41.0 reduce-scatter.18
  589.2 40.8 reduce-scatter.20
  632.5 40.9 reduce-scatter.22
  675.9 40.9 reduce-scatter.16
where the time goes:
time: 750 us; the launch traced here: 741 us
  waiting for transfers between devices  404 us (54%)
  matrix products  136 us (18%)
  blocking collectives  110 us (15%)
  local copies, waits for them, and re-layouts  38.6 us (5%)
  starting transfers between devices  20.2 us (3%)
  other arithmetic  17.8 us (2%)
  between operations  14.8 us (2%)
    all_gather x4, waiting for transfers between devices, on_device(): v_all = lax.all_gather(chip_v[:, cols], 'sc', axis=0, tiled=True)  159 us
    reduce_scatter x4, waiting for transfers between devices, on_device(): lax.psum_scatter(value_term.astype(jnp.bfloat16).reshape(seq_total, group...  154 us
    psum x1, blocking collectives, on_device(): filter_gradient = lax.psum(jnp.stack(filter_rows, 0), ('dp', 'sc', 'core'))  81.5 us
    all_gather x4, waiting for transfers between devices, on_device(): k_all = lax.all_gather(chip_k[:, cols], 'sc', axis=0, tiled=True)  57.5 us
    dot_general x4, matrix products, on_device(): jnp.einsum('htu,thd->uhd', dscore, q_part, preferred_element_type=jnp.flo...  38.7 us
    dot_general x4, matrix products, on_device(): jnp.einsum('htu,uhd->thd', dscore, k_part, preferred_element_type=jnp.flo...  32.2 us
    ppermute x2, waiting for transfers between devices, padded(): after = lax.ppermute(value[:width], SEQ, down)  28.2 us
    sub x4, matrix products, on_device(): raw = jnp.where(visible, jnp.exp(scores - row_top), 0.0)  24.9 us
  transfers between devices with their start and end apart: 23, of which 15 were waited for; matrix products, arithmetic and copies ran while one was open for 25% of the time, Pallas kernels for 0%

commit v1 on v0

--- a/solution.py
+++ b/solution.py
@@ -124,7 +124,8 @@
         moved = out_pad[tap_index : tap_index + tok_rows].astype(jnp.float32)
         conv_sum = conv_sum + filter_taps[tap_index] * moved
         filter_rows.append(jnp.sum(moved * local_gf, 0))
-    filter_gradient = lax.psum(jnp.stack(filter_rows, 0), ("dp", "sc", "core"))
+    x0 = jnp.stack(filter_rows, 0)
+    filter_gradient = jnp.sum(lax.all_gather(x0, ("dp", "sc", "core")), 0)
     conv_output = conv_sum.astype(jnp.bfloat16)
     return (
         conv_output[None],

time: 750 us -> 1180 us (1.57)
  waiting for transfers between devices: 404 us -> 902 us
  blocking collectives: 110 us -> 41.5 us
  starting transfers between devices: 20.2 us -> 7.6 us
    all_gather x0 -> x1, waiting for transfers between devices: none -> 418 us  [on_device(): filter_gradient = jnp.sum(lax.all_gather(x0, ('dp', 'sc', 'core')), 0)]
    psum x1 -> x0, blocking collectives: 81.5 us -> none  [on_device(): filter_gradient = lax.psum(jnp.stack(filter_rows, 0), ('dp', 'sc', 'core'))]
    reduce_scatter x4, waiting for transfers between devices: 0.03 us -> 57.8 us  [on_device(): lax.psum_scatter(key_term.astype(jnp.bfloat16).reshape(seq_total, group_w...]
    reduce_scatter x4, waiting for transfers between devices: 154 us -> 173 us  [on_device(): lax.psum_scatter(value_term.astype(jnp.bfloat16).reshape(seq_total, group...]
    all_to_all x2 -> x4, blocking collectives: 13.1 us -> 26.4 us  [from_chip_rows(): out = lax.all_to_all(split, 'core', 0, 2, tiled=True)]
    all_to_all x2 -> x0, starting transfers between devices: 12.5 us -> none  [from_chip_rows(): out = lax.all_to_all(split, 'core', 0, 2, tiled=True)]
  transfers between devices with their start and end apart: 23 -> 22, of which waited for: 15 -> 18; matrix products, arithmetic and copies ran while one was open for 25% -> 16% of each run, Pallas kernels for 0% -> 0%
where the time goes in v1:
time: 1180 us; the launch traced here: 1170 us
  waiting for transfers between devices  902 us (76%)
  matrix products  139 us (12%)
  blocking collectives  41.5 us (4%)
  local copies, waits for them, and re-layouts  38.7 us (3%)
  other arithmetic  23.7 us (2%)
  between operations  14.8 us (1%)
    all_gather x1, waiting for transfers between devices, on_device(): filter_gradient = jnp.sum(lax.all_gather(x0, ('dp', 'sc', 'core')), 0)  418 us
    reduce_scatter x4, waiting for transfers between devices, on_device(): lax.psum_scatter(value_term.astype(jnp.bfloat16).reshape(seq_total, group...  173 us
    all_gather x4, waiting for transfers between devices, on_device(): v_all = lax.all_gather(chip_v[:, cols], 'sc', axis=0, tiled=True)  158 us
    all_gather x4, waiting for transfers between devices, on_device(): k_all = lax.all_gather(chip_k[:, cols], 'sc', axis=0, tiled=True)  58.5 us
    reduce_scatter x4, waiting for transfers between devices, on_device(): lax.psum_scatter(key_term.astype(jnp.bfloat16).reshape(seq_total, group_w...  57.8 us
    dot_general x4, matrix products, on_device(): jnp.einsum('htu,thd->uhd', dscore, q_part, preferred_element_type=jnp.flo...  38.7 us
    ppermute x2, waiting for transfers between devices, padded(): after = lax.ppermute(value[:width], SEQ, down)  33.3 us
    dot_general x4, matrix products, on_device(): jnp.einsum('htu,uhd->thd', dscore, k_part, preferred_element_type=jnp.flo...  32.6 us
  transfers between devices with their start and end apart: 22, of which 18 were waited for; matrix products, arithmetic and copies ran while one was open for 16% of the time, Pallas kernels for 0%

profile of v1, /device:TPU:1, one launch (start us, length us, event | category | flops | bytes accessed | tf_op | source)
XLA Modules:
  0.0 1167.2 jit_solution(9703639769028915790)
XLA Ops:
  36.2 21.2 %collective-permute-done.2 = bf16[3,2048]{0,1:T(8,128)(2,1)S(1)} collective-permute-done((bf16[3,2048]{0,1:T(8,128)(2,1)}, bf16[3,2048]{0,1:T(8,128)(2,1)S(1)}, u32[]{:S(2)}, u32[]{:S(2)}) %collective-permute-start.2) | collective-permute-done | bytes 12320 | tf_op jit(solution)/shard_map/ppermute | solution.py:21
  71.0 33.9 %all-gather.18.cloned.1.call-done = bf16[2048,256]{1,0:T(8,128)(2,1)} async-done(((bf16[256,256]{1,0:T(8,128)(2,1)}), bf16[2048,256]{1,0:T(8,128)(2,1)}) %all-gather.18.cloned.1.call-update) | async-done | bytes 1048592 | tf_op jit(solution)/shard_map/all_gather | solution.py:74
  115.8 9.7 convolution_convert_fusion.2
  127.2 19.8 %all-gather.20.cloned.1.call-done = bf16[2048,256]{1,0:T(8,128)(2,1)} async-done(((bf16[256,256]{1,0:T(8,128)(2,1)}), bf16[2048,256]{1,0:T(8,128)(2,1)}) %all-gather.20.cloned.1.call-update) | async-done | bytes 1048592 | tf_op jit(solution)/shard_map/all_gather | solution.py:73
  149.3 41.2 %all-gather.22.cloned.1.call-done = bf16[2048,256]{1,0:T(8,128)(2,1)} async-done(((bf16[256,256]{1,0:T(8,128)(2,1)}), bf16[2048,256]{1,0:T(8,128)(2,1)}) %all-gather.22.cloned.1.call-update) | async-done | bytes 1048592 | tf_op jit(solution)/shard_map/all_gather | solution.py:74
  202.2 9.7 convolution_convert_fusion.1
  213.7 19.4 %all-gather.24.cloned.1.call-done = bf16[2048,256]{1,0:T(8,128)(2,1)} async-done(((bf16[256,256]{1,0:T(8,128)(2,1)}), bf16[2048,256]{1,0:T(8,128)(2,1)}) %all-gather.24.cloned.1.call-update) | async-done | bytes 1048592 | tf_op jit(solution)/shard_map/all_gather | solution.py:73
  235.3 41.3 %all-gather.26.cloned.1.call-done = bf16[2048,256]{1,0:T(8,128)(2,1)} async-done(((bf16[256,256]{1,0:T(8,128)(2,1)}), bf16[2048,256]{1,0:T(8,128)(2,1)}) %all-gather.26.cloned.1.call-update) | async-done | bytes 1048592 | tf_op jit(solution)/shard_map/all_gather | solution.py:74
  289.4 9.7 convolution_convert_fusion
  300.2 19.3 %all-gather.12.cloned.1.call-done = bf16[2048,256]{1,0:T(8,128)(2,1)} async-done(((bf16[256,256]{1,0:T(8,128)(2,1)}), bf16[2048,256]{1,0:T(8,128)(2,1)}) %all-gather.12.cloned.1.call-update) | async-done | bytes 1048592 | tf_op jit(solution)/shard_map/all_gather | solution.py:73
  321.7 41.5 %all-gather.14.cloned.1.call-done = bf16[2048,256]{1,0:T(8,128)(2,1)} async-done(((bf16[256,256]{1,0:T(8,128)(2,1)}), bf16[2048,256]{1,0:T(8,128)(2,1)}) %all-gather.14.cloned.1.call-update) | async-done | bytes 1048592 | tf_op jit(solution)/shard_map/all_gather | solution.py:74
  375.8 9.7 convolution_convert_fusion.3
  414.1 9.1 all_to_all.123
  425.9 12.1 %collective-permute-done.1 = bf16[3,2048]{0,1:T(8,128)(2,1)S(1)} collective-permute-done((bf16[3,2048]{0,1:T(8,128)(2,1)S(1)}, bf16[3,2048]{0,1:T(8,128)(2,1)S(1)}, u32[]{:S(2)}, u32[]{:S(2)}) %collective-permute-start.1) | collective-permute-done | bytes 12320 | tf_op jit(solution)/shard_map/ppermute | solution.py:21
  442.1 8.2 fusion.91
  450.6 8.2 fusion.94
  485.9 14.4 %reduce-scatter.15.cloned.1.call-done = bf16[256,256]{0,1:T(8,128)(2,1)} async-done(((bf16[2048,256]{0,1:T(8,128)(2,1)}), bf16[256,256]{0,1:T(8,128)(2,1)}) %reduce-scatter.15.cloned.1.call-update) | async-done | bytes 131088 | tf_op jit(solution)/shard_map/reduce_scatter | solution.py:100
  500.3 43.4 %reduce-scatter.9.cloned.1.call-done = bf16[256,256]{0,1:T(8,128)(2,1)} async-done(((bf16[2048,256]{0,1:T(8,128)(2,1)}), bf16[256,256]{0,1:T(8,128)(2,1)}) %reduce-scatter.9.cloned.1.call-update) | async-done | bytes 131088 | tf_op jit(solution)/shard_map/reduce_scatter | solution.py:100
  545.0 42.2 %reduce-scatter.19.cloned.1.call-done = bf16[256,256]{0,1:T(8,128)(2,1)} async-done(((bf16[2048,256]{0,1:T(8,128)(2,1)}), bf16[256,256]{0,1:T(8,128)(2,1)}) %reduce-scatter.19.cloned.1.call-update) | async-done | bytes 131088 | tf_op jit(solution)/shard_map/reduce_scatter | solution.py:108
  587.3 43.4 %reduce-scatter.21.cloned.1.call-done = bf16[256,256]{0,1:T(8,128)(2,1)} async-done(((bf16[2048,256]{0,1:T(8,128)(2,1)}), bf16[256,256]{0,1:T(8,128)(2,1)}) %reduce-scatter.21.cloned.1.call-update) | async-done | bytes 131088 | tf_op jit(solution)/shard_map/reduce_scatter | solution.py:108
  630.6 43.4 %reduce-scatter.23.cloned.1.call-done = bf16[256,256]{0,1:T(8,128)(2,1)} async-done(((bf16[2048,256]{0,1:T(8,128)(2,1)}), bf16[256,256]{0,1:T(8,128)(2,1)}) %reduce-scatter.23.cloned.1.call-update) | async-done | bytes 131088 | tf_op jit(solution)/shard_map/reduce_scatter | solution.py:108
  674.0 43.5 %reduce-scatter.17.cloned.1.call-done = bf16[256,256]{0,1:T(8,128)(2,1)} async-done(((bf16[2048,256]{0,1:T(8,128)(2,1)}), bf16[256,256]{0,1:T(8,128)(2,1)}) %reduce-scatter.17.cloned.1.call-update) | async-done | bytes 131088 | tf_op jit(solution)/shard_map/reduce_scatter | solution.py:108
  718.9 9.2 all_to_all.125
  734.8 418.1 %all-gather.28.cloned.1.call-done = f32[256,7,2048]{2,1,0:T(8,128)} async-done(((f32[1,7,2048]{2,1,0:T(8,128)}), f32[256,7,2048]{2,1,0:T(8,128)}) %all-gather.28.cloned.1.call-update) | async-done | bytes 14680080 | tf_op jit(solution)/shard_map/all_gather | solution.py:128
  (182 shorter events, 180.9 us)
Async XLA Ops:
  7.2 62.3 %all-gather.16.cloned.1.call-start = ((), (), s32[]{:S(2)}) async-start(), calls=%async_computation.18 | async-start | bytes 1179648 | tf_op jit(solution)/shard_map/all_gather | solution.py:73
  16.8 88.0 %all-gather.18.cloned.1.call-start = ((), (), s32[]{:S(2)}) async-start(), calls=%async_computation.19 | async-start | bytes 1179648 | tf_op jit(solution)/shard_map/all_gather | solution.py:74
  22.4 124.7 %all-gather.20.cloned.1.call-start = ((), (), s32[]{:S(2)}) async-start(), calls=%async_computation.20 | async-start | bytes 1179648 | tf_op jit(solution)/shard_map/all_gather | solution.py:73
  23.1 167.5 %all-gather.22.cloned.1.call-start = ((), (), s32[]{:S(2)}) async-start(), calls=%async_computation.21 | async-start | bytes 1179648 | tf_op jit(solution)/shard_map/all_gather | solution.py:74
  23.7 209.4 %all-gather.24.cloned.1.call-start = ((), (), s32[]{:S(2)}) async-start(), calls=%async_computation.22 | async-start | bytes 1179648 | tf_op jit(solution)/shard_map/all_gather | solution.py:73
  24.3 252.4 %all-gather.26.cloned.1.call-start = ((), (), s32[]{:S(2)}) async-start(), calls=%async_computation.23 | async-start | bytes 1179648 | tf_op jit(solution)/shard_map/all_gather | solution.py:74
  24.8 294.7 %all-gather.12.cloned.1.call-start = ((), (), s32[]{:S(2)}) async-start(), calls=%async_computation.16 | async-start | bytes 1179648 | tf_op jit(solution)/shard_map/all_gather | solution.py:73
  26.6 8.0 all-to-all-start
  30.4 332.8 %all-gather.14.cloned.1.call-start = ((), (), s32[]{:S(2)}) async-start(), calls=%async_computation.17 | async-start | bytes 1179648 | tf_op jit(solution)/shard_map/all_gather | solution.py:74
  31.7 25.8 %collective-permute-start.2 = (bf16[3,2048]{0,1:T(8,128)(2,1)}, bf16[3,2048]{0,1:T(8,128)(2,1)S(1)}, u32[]{:S(2)}, u32[]{:S(2)}) collective-permute-start(bf16[3,2048]{0,1:T(8,128)(2,1)} %get-tuple-element.38), channel_id=1, source_target_pairs={{1,0},{2,1},{3,2},{4,3},{5,4},{6,5},{7,6},{8,7},{9,8},{10,9},{11,1... | collective-permute-start | bytes 36872 | tf_op jit(solution)/shard_map/ppermute | solution.py:21
  31.8 26.3 %collective-permute-start.3 = (bf16[3,2048]{0,1:T(8,128)(2,1)S(1)}, bf16[3,2048]{0,1:T(8,128)(2,1)}, u32[]{:S(2)}, u32[]{:S(2)}) collective-permute-start(bf16[3,2048]{0,1:T(8,128)(2,1)S(1)} %get-tuple-element.39), channel_id=1, source_target_pairs={{0,1},{1,2},{2,3},{3,4},{4,5},{5,6},{6,7},{7,8},{8,9},{9,10},{10,1... | collective-permute-start | bytes 36872 | tf_op jit(solution)/shard_map/ppermute | solution.py:20
  33.5 452.4 %reduce-scatter.11.cloned.1.call-start = ((), (), s32[]{:S(2)}) async-start(), calls=%async_computation.25 | async-start | bytes 1179648 | tf_op jit(solution)/shard_map/reduce_scatter | solution.py:100
  71.0 44.8 %copy-start.2 = (bf16[2048,256]{0,1:T(8,128)(2,1)}, bf16[2048,256]{0,1:T(8,128)(2,1)S(1)}, u32[]{:S(2)}) copy-start(bf16[2048,256]{0,1:T(8,128)(2,1)S(1)} %copy.289) | copy-start | bytes 3145732
  125.5 360.4 %reduce-scatter.13.cloned.1.call-start = ((), (), s32[]{:S(2)}) async-start(), calls=%async_computation.26 | async-start | bytes 1179648 | tf_op jit(solution)/shard_map/reduce_scatter | solution.py:100
  211.9 288.5 %reduce-scatter.15.cloned.1.call-start = ((), (), s32[]{:S(2)}) async-start(), calls=%async_computation.27 | async-start | bytes 1179648 | tf_op jit(solution)/shard_map/reduce_scatter | solution.py:100
  299.1 244.6 %reduce-scatter.9.cloned.1.call-start = ((), (), s32[]{:S(2)}) async-start(), calls=%async_computation.24 | async-start | bytes 1179648 | tf_op jit(solution)/shard_map/reduce_scatter | solution.py:100
  321.7 47.7 %copy-start.10 = (bf16[256,256]{0,1:T(8,128)(2,1)S(1)}, bf16[256,256]{0,1:T(8,128)(2,1)}, u32[]{:S(2)}) copy-start(bf16[256,256]{0,1:T(8,128)(2,1)} %copy.277) | copy-start | bytes 393220
  385.6 201.7 %reduce-scatter.19.cloned.1.call-start = ((), (), s32[]{:S(2)}) async-start(), calls=%async_computation.29 | async-start | bytes 1179648 | tf_op jit(solution)/shard_map/reduce_scatter | solution.py:108
  389.4 241.2 %reduce-scatter.21.cloned.1.call-start = ((), (), s32[]{:S(2)}) async-start(), calls=%async_computation.30 | async-start | bytes 1179648 | tf_op jit(solution)/shard_map/reduce_scatter | solution.py:108
  393.3 280.8 %reduce-scatter.23.cloned.1.call-start = ((), (), s32[]{:S(2)}) async-start(), calls=%async_computation.31 | async-start | bytes 1179648 | tf_op jit(solution)/shard_map/reduce_scatter | solution.py:108
  397.1 320.4 %reduce-scatter.17.cloned.1.call-start = ((), (), s32[]{:S(2)}) async-start(), calls=%async_computation.28 | async-start | bytes 1179648 | tf_op jit(solution)/shard_map/reduce_scatter | solution.py:108
  407.5 745.4 %all-gather.28.cloned.1.call-start = ((), (), s32[]{:S(2)}) async-start(), calls=%async_computation.32 | async-start | bytes 16842752 | tf_op jit(solution)/shard_map/all_gather | solution.py:128
  423.9 1.6 collective-permute-start
  424.4 13.6 %collective-permute-start.1 = (bf16[3,2048]{0,1:T(8,128)(2,1)S(1)}, bf16[3,2048]{0,1:T(8,128)(2,1)S(1)}, u32[]{:S(2)}, u32[]{:S(2)}) collective-permute-start(bf16[3,2048]{0,1:T(8,128)(2,1)S(1)} %bitcast.223), channel_id=1, source_target_pairs={{1,0},{2,1},{3,2},{4,3},{5,4},{6,5},{7,6},{8,7},{9,8},{10,9},{11,1... | collective-permute-start | bytes 36872 | tf_op jit(solution)/shard_map/ppermute | solution.py:21
  (19 other events, 143.9 us)
Sparse Core Ops, SparseCore 0:
  17.0 45.7 all-gather.15
  64.5 40.3 all-gather.17
  106.7 40.3 all-gather.19
  148.7 41.8 all-gather.21
  192.2 40.8 all-gather.23
  235.3 41.2 all-gather.25
  278.4 41.0 all-gather.11
  321.9 41.3 all-gather.13
  365.8 41.8 reduce-scatter.10
  410.0 47.2 reduce-scatter.12
  459.9 40.3 reduce-scatter.14
  502.7 40.9 reduce-scatter.8
  546.2 40.9 reduce-scatter.18
  589.6 40.9 reduce-scatter.20
  633.0 40.9 reduce-scatter.22
  676.4 41.0 reduce-scatter.16
  719.9 433.0 all-gather.27
